TPU v7x, 512 devices: a whole 4x8x8 slice. The times are simulated.
512 devices in a mesh: req: 64 (over z, x, core), tp: 8 (over y).
Axes of the slice: x: 4, y: 8, z: 8, core: 2. Of those that a mesh axis runs over, the one named last changes fastest.
Arguments:
- q_new: bfloat16 [4096, 5120], P('req', 'tp'), may hold values from -6 to 6
- k_new: bfloat16 [4096, 1024], P('req', 'tp'), may hold values from -15 to 15
- v_new: bfloat16 [4096, 1024], P('req', 'tp'), may hold values from -6 to 6
- k_cache: bfloat16 [1024, 128, 1024], P('req', None, 'tp'), may hold values from -16 to 16
- v_cache: bfloat16 [1024, 128, 1024], P('req', None, 'tp'), may hold values from -6 to 6
- lengths: int32 [32], replicated, may hold values from 1 to 4096, as said below
- page_table: int32 [32, 32], replicated, may hold values from -1 to 1023, as said below
- w_out: bfloat16 [5120, 5120], P('req', 'tp'), may hold values from -0.078125 to 0.078125
Outputs:
- attn_out: bfloat16 [4096, 5120], P('req')
Inputs may be any that keep to these rules, and one draw needn't show every extreme that they name: `lengths`: the last request, 31, has exactly 4096 cached tokens; every request has at least one. `page_table`: request r uses ceil(lengths[r] / 128) logical pages. Its first ceil(ceil(lengths[r] / 128) / 2) logical pages lie among global pages 2r * 16 to (2r + 1) * 16 - 1, the rest among (2r + 1) * 16 to (2r + 2) * 16 - 1; distinct logical pages use distinct global pages; entries past a request's last page are -1.
All inputs are finite; a program needn't handle non-finite values.
Results may differ from a plain program's by a relative error of at most 0.024.
Values may be sent and summed in bfloat16 or wider, within the bound.
No kernel may reach another device: no remote copies, remote signals or barrier semaphores. Data moves between devices by JAX's collectives and lax.ppermute only.
A program may use at most 64 MiB of HBM per device.

v0:
```python
import math
import jax
import jax.numpy as jnp
from jax import lax
from jax.sharding import Mesh
from jax.sharding import PartitionSpec as P

HD = 128
GROUP = 5
ROWS = ("z", "x", "core")
ROPE_BASE = 1000000.0
FLOOR_SCORE = -1e30


def from_partner(value, axis, distance):
    return lax.ppermute(value, axis, [(i, i ^ 1 << distance) for i in range(lax.axis_size(axis))])


def rotate(values, places):
    inverse = 1.0 / ROPE_BASE ** (jnp.arange(0, HD, 2).astype(jnp.float32) / HD)
    angles = places.astype(jnp.float32)[:, None] * inverse[None, :]
    cosine = jnp.concatenate([jnp.cos(angles), jnp.cos(angles)], axis=-1)[:, None, :]
    sine = jnp.concatenate([jnp.sin(angles), jnp.sin(angles)], axis=-1)[:, None, :]
    first_half = values[..., : HD // 2]
    second_half = values[..., HD // 2 :]
    turned = jnp.concatenate([-second_half, first_half], axis=-1)
    return values * cosine + turned * sine


def absorb(state, queries, block_keys, block_values, allowed, scale):
    running_max, running_sum, output = state
    scores = (
        jnp.einsum("qcgd,kcd->cgqk", queries, block_keys, preferred_element_type=jnp.float32)
        * scale
    )
    scores = jnp.where(allowed[None, None], scores, FLOOR_SCORE)
    new_max = jnp.maximum(running_max, jnp.max(scores, axis=-1))
    factor = jnp.exp(running_max - new_max)
    weights = jnp.where(allowed[None, None], jnp.exp(scores - new_max[..., None]), 0.0)
    running_sum = running_sum * factor + jnp.sum(weights, axis=-1)
    mixed = jnp.einsum(
        "cgqk,kcd->qcgd",
        weights.astype(jnp.bfloat16),
        block_values,
        preferred_element_type=jnp.float32,
    )
    output = output * jnp.transpose(factor, (2, 0, 1))[..., None] + mixed
    return (new_max, running_sum, output)


def output_rows(w_out):
    parts = lax.axis_size("tp")
    rows, width = w_out.shape
    share = rows // parts
    pieces = lax.all_to_all(w_out.reshape(parts, share, width), "tp", 0, 0, tiled=True)
    mine = jnp.transpose(pieces, (1, 0, 2))
    near = lax.all_gather(mine, "z", axis=0, tiled=True)
    return (lax.all_gather(near, ("x", "core"), axis=0, tiled=True), share)


def shards(q_new, k_new, v_new, k_cache, v_cache, lengths, page_table, w_out):
    own_rows = q_new.shape[0]
    all_rows = 2 * own_rows
    local_heads = k_new.shape[1] // HD
    pages_local = k_cache.shape[0]
    page_rows = k_cache.shape[1]
    scale = 1.0 / math.sqrt(HD)
    weights_mine, share = output_rows(w_out)
    device_row = (lax.axis_index("z") * lax.axis_size("x") + lax.axis_index("x")) * lax.axis_size(
        "core"
    ) + lax.axis_index("core")
    parity = device_row % 2
    request = device_row // 2
    length = lengths[request]
    own_places = length + parity * own_rows + jnp.arange(own_rows)
    own_queries = rotate(
        q_new.reshape(own_rows, local_heads * GROUP, HD).astype(jnp.float32), own_places
    ).astype(jnp.bfloat16)
    own_keys = rotate(
        k_new.reshape(own_rows, local_heads, HD).astype(jnp.float32), own_places
    ).astype(jnp.bfloat16)
    own_values = v_new.reshape(own_rows, local_heads, HD)
    query_heads = own_queries.shape[1]
    peer_pack = from_partner(
        jnp.concatenate([own_queries, own_keys, own_values], axis=1), "core", 0
    )
    peer_queries = peer_pack[:, :query_heads]
    peer_keys = peer_pack[:, query_heads : query_heads + local_heads]
    peer_values = peer_pack[:, query_heads + local_heads :]

    def ordered(mine, theirs):
        return jnp.where(
            parity == 0,
            jnp.concatenate([mine, theirs], axis=0),
            jnp.concatenate([theirs, mine], axis=0),
        )

    queries = ordered(own_queries, peer_queries).reshape(all_rows, local_heads, GROUP, HD)
    fresh_keys = ordered(own_keys, peer_keys)
    fresh_values = ordered(own_values, peer_values)
    state = (
        jnp.full((local_heads, GROUP, all_rows), FLOOR_SCORE, jnp.float32),
        jnp.zeros((local_heads, GROUP, all_rows), jnp.float32),
        jnp.zeros((all_rows, local_heads, GROUP, HD), jnp.float32),
    )
    token_index = jnp.arange(all_rows)
    causal = (token_index[None, :] <= token_index[:, None]) & (parity == 1)
    state = absorb(state, queries, fresh_keys, fresh_values, causal, scale)
    page_count = (length + page_rows - 1) // page_rows
    even_pages = (page_count + 1) // 2
    first_page = jnp.where(parity == 0, 0, even_pages)
    last_page = jnp.where(parity == 0, even_pages, page_count)
    table_row = page_table[request]
    logical = jnp.arange(table_row.shape[0])
    in_range = (logical >= first_page) & (logical < last_page)
    offset = device_row * pages_local
    slot_ids = jnp.arange(pages_local)
    match = in_range[:, None] & (table_row[:, None] - offset == slot_ids[None, :])
    used = jnp.any(match, axis=0)
    base = jnp.sum(jnp.where(match, logical[:, None], 0), axis=0) * page_rows
    key_places = (base[:, None] + jnp.arange(page_rows)[None, :]).reshape(-1)
    usable = jnp.repeat(used, page_rows) & (key_places < length)
    allowed = jnp.broadcast_to(usable[None, :], (all_rows, pages_local * page_rows))
    pool_keys = k_cache.reshape(pages_local * page_rows, local_heads, HD)
    pool_values = v_cache.reshape(pages_local * page_rows, local_heads, HD)
    half = pool_keys.shape[0] // 2
    for start in (0, half):
        state = absorb(
            state,
            queries,
            pool_keys[start : start + half],
            pool_values[start : start + half],
            allowed[:, start : start + half],
            scale,
        )
    running_max, running_sum, output = state
    peer_start = (1 - parity) * own_rows
    own_start = parity * own_rows
    outgoing = (
        lax.dynamic_slice_in_dim(output, peer_start, own_rows, 0),
        lax.dynamic_slice_in_dim(running_max, peer_start, own_rows, 2),
        lax.dynamic_slice_in_dim(running_sum, peer_start, own_rows, 2),
    )
    outgoing = jnp.concatenate(
        [
            outgoing[0].astype(jnp.bfloat16),
            jnp.transpose(outgoing[1], (2, 0, 1))[..., None].astype(jnp.bfloat16),
            jnp.transpose(outgoing[2], (2, 0, 1))[..., None].astype(jnp.bfloat16),
        ],
        axis=-1,
    )
    incoming = from_partner(outgoing, "core", 0).astype(jnp.float32)
    other_output = incoming[..., :HD]
    other_max = jnp.transpose(incoming[..., HD], (1, 2, 0))
    other_sum = jnp.transpose(incoming[..., HD + 1], (1, 2, 0))
    mine_output = lax.dynamic_slice_in_dim(output, own_start, own_rows, 0)
    mine_max = lax.dynamic_slice_in_dim(running_max, own_start, own_rows, 2)
    mine_sum = lax.dynamic_slice_in_dim(running_sum, own_start, own_rows, 2)
    joint_max = jnp.maximum(mine_max, other_max)
    mine_factor = jnp.exp(mine_max - joint_max)
    other_factor = jnp.exp(other_max - joint_max)
    joint_sum = mine_sum * mine_factor + other_sum * other_factor
    joint_output = (
        mine_output * jnp.transpose(mine_factor, (2, 0, 1))[..., None]
        + other_output * jnp.transpose(other_factor, (2, 0, 1))[..., None]
    )
    attention = (
        (joint_output / jnp.transpose(joint_sum, (2, 0, 1))[..., None])
        .reshape(own_rows, local_heads * GROUP * HD)
        .astype(jnp.bfloat16)
    )
    full_rows = lax.all_gather(attention[:, None], "tp", axis=1, tiled=True)
    projected = lax.dot_general(
        full_rows, weights_mine, (((1, 2), (1, 2)), ((), ())), preferred_element_type=jnp.float32
    )
    depth = lax.axis_size("z")
    projected = projected.reshape(own_rows, -1, depth, share)
    projected = jnp.transpose(projected, (0, 2, 1, 3)).reshape(own_rows, -1, share)
    projected = projected.astype(jnp.bfloat16)
    gathered = lax.all_gather(projected, "tp", axis=2, tiled=True)
    return gathered.reshape(own_rows, -1)


def solution(mesh):
    in_specs = (
        P(ROWS, "tp"),
        P(ROWS, "tp"),
        P(ROWS, "tp"),
        P(ROWS, None, "tp"),
        P(ROWS, None, "tp"),
        P(),
        P(),
        P(ROWS, "tp"),
    )
    out_specs = P(ROWS, None)
    rows, parts = mesh.devices.shape
    cores = 2
    depth = 4 if rows % (4 * cores) == 0 else 1
    split = Mesh(mesh.devices.reshape(depth, rows // (depth * cores), cores, parts), ROWS + ("tp",))
    return jax.shard_map(
        shards, mesh=split, in_specs=in_specs, out_specs=out_specs, check_vma=False
    )
```

profile of v0, /device:TPU:6, one launch (start us, length us, event | category | flops | bytes accessed | tf_op | source)
XLA Modules:
  0.0 135.1 jit_solution(9151260461402743674)
XLA Ops:
  6.5 0.0 copy-start.3
  6.5 0.0 copy-start.6
  6.5 0.0 copy-start.5
  6.5 0.0 all-gather.2.cloned.1.call-start
  6.6 1.0 reshape.452
  7.6 16.7 %all_to_all.5 = bf16[8,10,640]{2,1,0:T(8,128)(2,1)S(1)} all-to-all(bf16[8,10,640]{2,1,0:T(8,128)(2,1)S(1)} %reshape.452), channel_id=1, replica_groups=mesh['z'=4,'x'=8,'core'=2,'tp'=8] {'tp'}, dimensions={0} | all-to-all | bytes 204800 | tf_op jit(solution)/shard_map/all_to_all | solution.py:55
  24.2 0.0 copy-start.1
  24.3 21.0 %all_gather.13 = bf16[40,8,640]{2,1,0:T(8,128)(2,1)S(1)} all-gather(bf16[10,8,640]{2,1,0:T(8,128)(2,1)S(1)} %copy.92), channel_id=1, replica_groups=mesh['z'=4,'x'=8,'core'=2,'tp'=8] {'z'}, dimensions={0}, use_global_device_ids=true | all-gather | bytes 512000 | tf_op jit(solution)/shard_map/all_gather | solution.py:57
  45.3 0.8 copy.93
  46.0 0.0 copy-start.2
  46.1 0.0 all-gather.2.cloned.1.call-update
  46.1 0.0 copy-done.3
  46.1 0.1 reshape.454
  46.2 0.0 copy-done.6
  46.2 0.6 dynamic_slice.24
  47.5 0.0 copy-done.4
  47.5 0.2 multiply_cosine_fusion
  47.7 0.1 fusion.54
  47.8 0.1 pad_maximum_fusion.2
  48.0 0.0 copy-done.5
  48.0 0.1 slice_negate_fusion
  48.1 0.1 fusion.41
  48.3 0.1 pad_maximum_fusion.1
  48.4 1.9 %collective-permute-start = (bf16[64,7,128]{2,1,0:T(8,128)(2,1)S(1)}, bf16[64,7,128]{2,1,0:T(8,128)(2,1)S(1)}, u32[]{:S(2)}, u32[]{:S(2)}) collective-permute-start(bf16[64,7,128]{2,1,0:T(8,128)(2,1)S(1)} %pad_maximum_fusion.1), channel_id=1, source_target_pairs={{0,8},{8,0},{1,9},{9,1},{2,10},{10,2},{3,11},{11,3},{4,12},{12,4},... | collective-permute-start | bytes 344072 | tf_op jit(solution)/shard_map/ppermute | solution.py:16
  51.1 0.7 fusion.97
  51.8 0.1 fusion.77
  51.9 0.1 select_reduce_fusion
  52.0 0.7 fusion.79
  52.7 0.0 copy-done.1
  52.8 0.0 copy-done.2
  52.8 0.8 fusion.110
  53.6 0.0 collective-permute-done
  53.6 0.1 fusion.112
  53.7 0.1 maximum_select_fusion
  53.9 0.2 fusion.113
  54.1 0.6 fusion.2
  54.7 0.0 copy-start
  54.7 0.6 fusion.3
  55.4 0.1 fusion.38
  55.4 1.5 %fusion.4 = (f32[5,128]{1,0:T(8,128)S(1)}, f32[5,128]{1,0:T(8,128)S(1)}) fusion(f32[128,5,1024]{2,0,1:T(8,128)S(1)} %get-tuple-element.38, f32[5,128]{1,0:T(8,128)S(1)} %get-tuple-element.10, pred[1024]{0:T(1024)(128)(4,1)S(1)} %get-tuple-element.8, f32[5,128]{1,0:T(8,128)S(1)} %get-tuple-element.9, f32[128,5,1024]{2,0,1:T(8,128)S(1)} %get-tuple-element.36, ...), kind=kLoop, calls=%fused_computation.8 | loop fusion | flops 6552320 | bytes 5255168 | tf_op jit(solution)/shard_map/reduce_sum | solution.py:40
  56.9 0.0 copy-done
  57.0 0.1 fusion.90
  57.0 0.1 copy.87
  57.2 0.1 fusion.91
  57.3 0.1 copy.88
  57.4 0.3 fusion.35
  57.7 2.5 %fusion.31 = f32[128,1,5,128]{3,0,2,1:T(8,128)S(1)} fusion(f32[128,1,5,128]{3,0,2,1:T(8,128)S(1)} %fusion.35, bf16[1024,128,1]{1,0,2:T(8,128)(2,1)} %bitcast.311, f32[128,5,1024]{2,0,1:T(8,128)} %copy-done, f32[5,128]{1,0:T(8,128)S(1)} %get-tuple-element.10, pred[1024]{0:T(1024)(128)(4,1)S(1)} %get-tuple-element.8, f32[128,5]{0,1:T(8,128)S(1)} %get-tuple-element.24), kind=kOutput, calls=%fused_computation.27 | convolution fusion | flops 171212800 | bytes 3545088 | tf_op jit(solution)/shard_map/cgqk,kcd->qcgd/dot_general | solution.py:41
  60.2 0.7 fusion.28
  61.0 0.1 pad_maximum_fusion
  61.1 2.4 %collective-permute-start.1 = (bf16[64,1,5,130]{3,0,2,1:T(8,128)(2,1)S(1)}, bf16[64,1,5,130]{3,0,2,1:T(8,128)(2,1)S(1)}, u32[]{:S(2)}, u32[]{:S(2)}) collective-permute-start(bf16[64,1,5,130]{3,0,2,1:T(8,128)(2,1)S(1)} %pad_maximum_fusion), channel_id=1, source_target_pairs={{0,8},{8,0},{1,9},{9,1},{2,10},{10,2},{3,11},{11,3},{4,12},{12,4},... | collective-permute-start | bytes 249608 | tf_op jit(solution)/shard_map/ppermute | solution.py:16
  63.5 1.0 collective-permute-done.1
  64.5 0.2 slice_reduce_fusion.1
  64.8 0.1 fusion.95
  64.8 0.2 copy_bitcast_fusion
  65.1 25.7 %all_gather.12 = bf16[64,8,640]{2,0,1:T(8,128)(2,1)S(1)} all-gather(bf16[64,1,640]{2,0,1:T(8,128)(2,1)S(1)} %copy_bitcast_fusion), channel_id=1, replica_groups=mesh['z'=4,'x'=8,'core'=2,'tp'=8] {'tp'}, dimensions={1}, use_global_device_ids=true | all-gather | bytes 737280 | tf_op jit(solution)/shard_map/all_gather | solution.py:172
  90.7 0.0 all-gather.2.cloned.1.call-done
  90.7 4.9 %fusion.37 = bf16[64,640]{1,0:T(8,128)(2,1)S(1)} fusion(bf16[64,8,640]{2,0,1:T(8,128)(2,1)S(1)} %all_gather.12, bf16[640,8,640]{2,0,1:T(8,128)(2,1)} %all-gather.2.cloned.1.call-done), kind=kOutput, calls=%fused_computation.32 | convolution fusion | flops 419471360 | bytes 7290880 | tf_op jit(solution)/shard_map/dot_general | solution.py:173
  95.7 0.2 copy.94
  95.8 0.1 convert_element_type.134
  95.9 0.1 copy.95
  96.0 0.1 copy.96
  96.2 27.6 %all_gather.15 = bf16[64,64,80]{1,0,2:T(8,128)(2,1)S(1)} all-gather(bf16[64,64,10]{1,0,2:T(8,128)(2,1)S(1)} %copy.96), channel_id=1, replica_groups=mesh['z'=4,'x'=8,'core'=2,'tp'=8] {'tp'}, dimensions={2}, use_global_device_ids=true | all-gather | bytes 737280 | tf_op jit(solution)/shard_map/all_gather | solution.py:180
  123.8 1.5 %copy.97 = bf16[64,64,80]{2,1,0:T(8,128)(2,1)S(1)} copy(bf16[64,64,80]{1,0,2:T(8,128)(2,1)S(1)} %all_gather.15) | data formatting | bytes 1310720 | tf_op jit(solution)/shard_map/all_gather | solution.py:180
  125.3 2.9 %reshape.453 = bf16[64,5120]{1,0:T(8,128)(2,1)} reshape(bf16[64,64,80]{2,1,0:T(8,128)(2,1)S(1)} %copy.97) | data formatting | bytes 1310720 | tf_op jit(solution)/shard_map/reshape | solution.py:181
  (19 shorter events, 0.3 us)
Async XLA Ops:
  6.5 39.6 %copy-start.3 = (bf16[64,640]{1,0:T(8,128)(2,1)S(1)}, bf16[64,640]{1,0:T(8,128)(2,1)}, u32[]{:S(2)}) copy-start(bf16[64,640]{1,0:T(8,128)(2,1)} %param.8) | copy-start | bytes 245764
  6.5 39.7 %copy-start.6 = (s32[32]{0:T(128)S(1)}, s32[32]{0:T(128)}, u32[]{:S(2)}) copy-start(s32[32]{0:T(128)} %param.13) | copy-start | bytes 388
  6.5 41.0 %copy-start.4 = (bf16[64,128]{1,0:T(8,128)(2,1)S(1)}, bf16[64,128]{1,0:T(8,128)(2,1)}, u32[]{:S(2)}) copy-start(bf16[64,128]{1,0:T(8,128)(2,1)} %param.9) | copy-start | bytes 49156
  6.5 41.4 %copy-start.5 = (bf16[64,128]{1,0:T(8,128)(2,1)S(1)}, bf16[64,128]{1,0:T(8,128)(2,1)}, u32[]{:S(2)}) copy-start(bf16[64,128]{1,0:T(8,128)(2,1)} %param.10) | copy-start | bytes 49156
  6.5 84.2 %all-gather.2.cloned.1.call-start = ((), (), s32[]{:S(2)}) async-start(), calls=%async_computation.1 | async-start | bytes 6963200 | tf_op jit(solution)/shard_map/all_gather | solution.py:58
  24.2 28.5 %copy-start.1 = (bf16[16,128,128]{2,1,0:T(8,128)(2,1)S(1)}, bf16[16,128,128]{2,1,0:T(8,128)(2,1)}, u32[]{:S(2)}) copy-start(bf16[16,128,128]{2,1,0:T(8,128)(2,1)} %param.11) | copy-start | bytes 1572868
  46.0 6.7 %copy-start.2 = (bf16[16,128,128]{2,1,0:T(8,128)(2,1)S(1)}, bf16[16,128,128]{2,1,0:T(8,128)(2,1)}, u32[]{:S(2)}) copy-start(bf16[16,128,128]{2,1,0:T(8,128)(2,1)} %param.12) | copy-start | bytes 1572868
  48.4 5.2 %collective-permute-start = (bf16[64,7,128]{2,1,0:T(8,128)(2,1)S(1)}, bf16[64,7,128]{2,1,0:T(8,128)(2,1)S(1)}, u32[]{:S(2)}, u32[]{:S(2)}) collective-permute-start(bf16[64,7,128]{2,1,0:T(8,128)(2,1)S(1)} %pad_maximum_fusion.1), channel_id=1, source_target_pairs={{0,8},{8,0},{1,9},{9,1},{2,10},{10,2},{3,11},{11,3},{4,12},{12,4},... | collective-permute-start | bytes 344072 | tf_op jit(solution)/shard_map/ppermute | solution.py:16
  54.7 2.2 %copy-start = (f32[128,5,1024]{2,0,1:T(8,128)}, f32[128,5,1024]{2,0,1:T(8,128)S(1)}, u32[]{:S(2)}) copy-start(f32[128,5,1024]{2,0,1:T(8,128)S(1)} %get-tuple-element.38) | copy-start | bytes 7864324
  61.1 3.4 %collective-permute-start.1 = (bf16[64,1,5,130]{3,0,2,1:T(8,128)(2,1)S(1)}, bf16[64,1,5,130]{3,0,2,1:T(8,128)(2,1)S(1)}, u32[]{:S(2)}, u32[]{:S(2)}) collective-permute-start(bf16[64,1,5,130]{3,0,2,1:T(8,128)(2,1)S(1)} %pad_maximum_fusion), channel_id=1, source_target_pairs={{0,8},{8,0},{1,9},{9,1},{2,10},{10,2},{3,11},{11,3},{4,12},{12,4},... | collective-permute-start | bytes 249608 | tf_op jit(solution)/shard_map/ppermute | solution.py:16
Sparse Core Ops, SparseCore 0:
  46.2 43.5 all-gather.1
where the time goes:
time: 135 us
  blocking collectives  90.9 us (67%)
  between operations  15.1 us (11%)
  matrix products  9.93 us (7%)
  local copies, waits for them, and re-layouts  9.09 us (7%)
  other arithmetic  4.56 us (3%)
  starting transfers between devices  4.38 us (3%)
    all_gather x1, blocking collectives, shards(): gathered = lax.all_gather(projected, 'tp', axis=2, tiled=True)  27.6 us
    all_gather x1, blocking collectives, shards(): full_rows = lax.all_gather(attention[:, None], 'tp', axis=1, tiled=True)  25.7 us
    all_gather x1, blocking collectives, output_rows(): near = lax.all_gather(mine, 'z', axis=0, tiled=True)  21 us
    all_to_all x1, blocking collectives, output_rows(): lax.all_to_all(w_out.reshape(parts, share, width), 'tp', 0, 0, tiled=True)  16.7 us
    dot_general x1, matrix products, shards(): lax.dot_general(full_rows, weights_mine, (((1, 2), (1, 2)), ((), ())), pr...  4.94 us
    ppermute x2, starting transfers between devices, from_partner(): lax.ppermute(value, axis, [(i, i ^ 1 << distance) for i in range(lax.axis...  4.35 us
    dot_general x3, matrix products, absorb(): jnp.einsum('cgqk,kcd->qcgd', weights.astype(jnp.bfloat16), block_values,...  3.52 us
    reshape x1, local copies, waits for them, and re-layouts, shards(): return gathered.reshape(own_rows, -1)  2.92 us
  transfers between devices with their start and end apart: 3, of which 1 were waited for; matrix products, arithmetic and copies ran while one was open for 9% of the time, Pallas kernels for 0%

commit v1 on v0

--- a/solution.py
+++ b/solution.py
@@ -10,6 +10,28 @@
 ROWS = ("z", "x", "core")
 ROPE_BASE = 1000000.0
 FLOOR_SCORE = -1e30
+
+
+def laid_out(tiles, dim):
+    tiles = jnp.moveaxis(tiles, 0, dim)
+    shape = tiles.shape
+    return tiles.reshape(*shape[:dim], shape[dim] * shape[dim + 1], *shape[dim + 2 :])
+
+
+def collect(value, axis, dim):
+    devices = lax.axis_size(axis)
+    pairs = [(i, (i + 1) % devices) for i in range(devices)]
+    back = [(b, a) for a, b in pairs]
+    lower, upper = ([], [])
+    for step in range(devices - 1):
+        if step % 2 == 0:
+            lower.append(lax.ppermute(lower[-1] if lower else value, axis, pairs))
+        else:
+            upper.append(lax.ppermute(upper[-1] if upper else value, axis, back))
+    blocks = jnp.stack([*lower[::-1], value, *upper])
+    shift = lax.axis_index(axis) - len(lower)
+    blocks = blocks[(jnp.arange(devices) - shift) % devices]
+    return laid_out(blocks, dim)
 
 
 def from_partner(value, axis, distance):
@@ -169,7 +191,7 @@
         .reshape(own_rows, local_heads * GROUP * HD)
         .astype(jnp.bfloat16)
     )
-    full_rows = lax.all_gather(attention[:, None], "tp", axis=1, tiled=True)
+    full_rows = collect(attention[:, None], "tp", 1)
     projected = lax.dot_general(
         full_rows, weights_mine, (((1, 2), (1, 2)), ((), ())), preferred_element_type=jnp.float32
     )

time: 135 us -> 151 us (1.12); the launches traced: 135 us -> 149 us
  blocking collectives: 90.9 us -> 65.8 us
  starting transfers between devices: 4.38 us -> 28.2 us
  waiting for transfers between devices: 1.02 us -> 8.93 us
  matrix products: 9.93 us -> 14.8 us
    all_gather x1 -> x0, blocking collectives: 25.7 us -> none  [shards(): full_rows = lax.all_gather(attention[:, None], 'tp', axis=1, tiled=True)]
    ppermute x0 -> x7, starting transfers between devices: none -> 23.9 us  [the longest x3 15.6 us: collect(): upper.append(lax.ppermute(upper[-1] if upper else value, axis, back))]
    ppermute x0 -> x7, waiting for transfers between devices: none -> 7.89 us  [the longest x4 6.24 us: collect(): lower.append(lax.ppermute(lower[-1] if lower else value, axis, pairs))]
    dot_general x1, matrix products: 4.94 us -> 9.76 us  [shards(): lax.dot_general(full_rows, weights_mine, (((1, 2), (1, 2)), ((), ())), pr...]
  transfers between devices with their start and end apart: 3 -> 10, of which waited for: 1 -> 6; matrix products, arithmetic and copies ran while one was open for 9% -> 11% of each run, Pallas kernels for 0% -> 0%
where the time goes in v1:
time: 151 us; the launch traced here: 149 us
  blocking collectives  65.8 us (44%)
  starting transfers between devices  28.2 us (19%)
  between operations  15.2 us (10%)
  matrix products  14.8 us (10%)
  local copies, waits for them, and re-layouts  10.4 us (7%)
  waiting for transfers between devices  8.93 us (6%)
  other arithmetic  6.03 us (4%)
    all_gather x1, blocking collectives, shards(): gathered = lax.all_gather(projected, 'tp', axis=2, tiled=True)  27.9 us
    all_gather x1, blocking collectives, output_rows(): near = lax.all_gather(mine, 'z', axis=0, tiled=True)  21.3 us
    all_to_all x1, blocking collectives, output_rows(): lax.all_to_all(w_out.reshape(parts, share, width), 'tp', 0, 0, tiled=True)  16.7 us
    ppermute x3, starting transfers between devices, collect(): upper.append(lax.ppermute(upper[-1] if upper else value, axis, back))  15.6 us
    dot_general x1, matrix products, shards(): lax.dot_general(full_rows, weights_mine, (((1, 2), (1, 2)), ((), ())), pr...  9.76 us
    ppermute x4, starting transfers between devices, collect(): lower.append(lax.ppermute(lower[-1] if lower else value, axis, pairs))  8.3 us
    ppermute x4, waiting for transfers between devices, collect(): lower.append(lax.ppermute(lower[-1] if lower else value, axis, pairs))  6.24 us
    ppermute x2, starting transfers between devices, from_partner(): lax.ppermute(value, axis, [(i, i ^ 1 << distance) for i in range(lax.axis...  4.3 us
  transfers between devices with their start and end apart: 10, of which 6 were waited for; matrix products, arithmetic and copies ran while one was open for 11% of the time, Pallas kernels for 0%

profile of v1, /device:TPU:6, one launch (start us, length us, event | category | flops | bytes accessed | tf_op | source)
XLA Modules:
  0.0 149.4 jit_solution(15456673577761612774)
XLA Ops:
  6.5 1.0 reshape.516
  7.5 16.7 %all_to_all.5 = bf16[8,10,640]{2,1,0:T(8,128)(2,1)S(1)} all-to-all(bf16[8,10,640]{2,1,0:T(8,128)(2,1)S(1)} %reshape.516), channel_id=1, replica_groups=mesh['z'=4,'x'=8,'core'=2,'tp'=8] {'tp'}, dimensions={0} | all-to-all | bytes 204800 | tf_op jit(solution)/shard_map/all_to_all | solution.py:77
  24.2 0.0 copy-start.2
  24.2 21.3 %all_gather.9 = bf16[40,8,640]{2,1,0:T(8,128)(2,1)} all-gather(bf16[10,8,640]{2,1,0:T(8,128)(2,1)S(1)} %copy.119), channel_id=1, replica_groups=mesh['z'=4,'x'=8,'core'=2,'tp'=8] {'z'}, dimensions={0}, use_global_device_ids=true | all-gather | bytes 512000 | tf_op jit(solution)/shard_map/all_gather | solution.py:79
  45.5 0.0 all-gather.2.cloned.1.call-update
  45.6 1.0 reshape.518
  46.5 1.2 dynamic_slice.24
  48.5 0.7 convert_bitcast_fusion
  49.2 0.2 multiply_cosine_fusion
  49.4 0.1 fusion.64
  49.5 0.8 pad_maximum_fusion.2
  50.4 0.1 slice_negate_fusion
  50.5 0.1 fusion.52
  50.7 0.1 pad_maximum_fusion.1
  50.8 1.9 %collective-permute-start = (bf16[64,7,128]{2,1,0:T(8,128)(2,1)S(1)}, bf16[64,7,128]{2,1,0:T(8,128)(2,1)S(1)}, u32[]{:S(2)}, u32[]{:S(2)}) collective-permute-start(bf16[64,7,128]{2,1,0:T(8,128)(2,1)S(1)} %pad_maximum_fusion.1), channel_id=1, source_target_pairs={{0,8},{8,0},{1,9},{9,1},{2,10},{10,2},{3,11},{11,3},{4,12},{12,4},... | collective-permute-start | bytes 344072 | tf_op jit(solution)/shard_map/ppermute | solution.py:38
  53.4 0.7 fusion.107
  54.1 0.1 fusion.87
  54.3 0.1 select_reduce_fusion
  54.4 0.7 fusion.89
  55.2 0.7 fusion.122
  56.0 0.0 collective-permute-done
  56.0 0.1 fusion.124
  56.1 0.1 maximum_select_fusion
  56.2 0.2 fusion.125
  56.5 0.6 fusion.4
  57.1 0.6 fusion.5
  57.7 0.1 fusion.49
  57.8 1.5 fusion.6
  59.3 0.1 fusion.100
  59.4 0.1 copy.113
  59.5 0.1 fusion.101
  59.6 0.1 copy.114
  59.8 0.3 fusion.40
  60.1 2.5 %fusion.36 = f32[128,1,5,128]{3,0,2,1:T(8,128)S(1)} fusion(f32[128,1,5,128]{3,0,2,1:T(8,128)S(1)} %fusion.40, bf16[1024,128,1]{1,0,2:T(8,128)(2,1)} %bitcast.342, f32[128,5,1024]{2,0,1:T(8,128)} %copy-done, f32[5,128]{1,0:T(8,128)S(1)} %get-tuple-element.10, pred[1024]{0:T(1024)(128)(4,1)S(1)} %get-tuple-element.8, f32[128,5]{0,1:T(8,128)S(1)} %get-tuple-element.24), kind=kOutput, calls=%fused_computation.31 | convolution fusion | flops 171212800 | bytes 3545088 | tf_op jit(solution)/shard_map/cgqk,kcd->qcgd/dot_general | solution.py:63
  62.6 0.7 fusion.33
  63.4 0.1 pad_maximum_fusion
  63.5 2.4 %collective-permute-start.1 = (bf16[64,1,5,130]{3,0,2,1:T(8,128)(2,1)S(1)}, bf16[64,1,5,130]{3,0,2,1:T(8,128)(2,1)S(1)}, u32[]{:S(2)}, u32[]{:S(2)}) collective-permute-start(bf16[64,1,5,130]{3,0,2,1:T(8,128)(2,1)S(1)} %pad_maximum_fusion), channel_id=1, source_target_pairs={{0,8},{8,0},{1,9},{9,1},{2,10},{10,2},{3,11},{11,3},{4,12},{12,4},... | collective-permute-start | bytes 249608 | tf_op jit(solution)/shard_map/ppermute | solution.py:38
  65.9 1.0 collective-permute-done.1
  66.9 0.2 slice_reduce_fusion.1
  67.1 0.1 fusion.105
  67.2 0.2 fusion.59
  67.4 2.6 %collective-permute-start.2 = (bf16[64,1,640]{2,0,1:T(8,128)(2,1)S(1)}, bf16[64,1,640]{2,0,1:T(8,128)(2,1)S(1)}, u32[]{:S(2)}, u32[]{:S(2)}) collective-permute-start(bf16[64,1,640]{2,0,1:T(8,128)(2,1)S(1)} %copy_bitcast_fusion), channel_id=1, source_target_pairs={{0,1},{1,2},{2,3},{3,4},{4,5},{5,6},{6,7},{7,0},{8,9},{9,10},{10,1... | collective-permute-start | bytes 245768 | tf_op jit(solution)/shard_map/ppermute | solution.py:28
  70.0 5.2 %collective-permute-done.2 = bf16[64,1,640]{2,0,1:T(8,128)(2,1)S(1)} collective-permute-done((bf16[64,1,640]{2,0,1:T(8,128)(2,1)S(1)}, bf16[64,1,640]{2,0,1:T(8,128)(2,1)S(1)}, u32[]{:S(2)}, u32[]{:S(2)}) %collective-permute-start.2) | collective-permute-done | bytes 81952 | tf_op jit(solution)/shard_map/ppermute | solution.py:28
  75.3 1.9 %collective-permute-start.3 = (bf16[64,1,640]{2,0,1:T(8,128)(2,1)S(1)}, bf16[64,1,640]{2,0,1:T(8,128)(2,1)S(1)}, u32[]{:S(2)}, u32[]{:S(2)}) collective-permute-start(bf16[64,1,640]{2,0,1:T(8,128)(2,1)S(1)} %collective-permute-done.2), channel_id=1, source_target_pairs={{0,1},{1,2},{2,3},{3,4},{4,5},{5,6},{6,7},{7,0},{8,9},{9,10},{10,1... | collective-permute-start | bytes 245768 | tf_op jit(solution)/shard_map/ppermute | solution.py:28
  77.2 5.1 %collective-permute-start.6 = (bf16[64,1,640]{2,0,1:T(8,128)(2,1)S(1)}, bf16[64,1,640]{2,0,1:T(8,128)(2,1)S(1)}, u32[]{:S(2)}, u32[]{:S(2)}) collective-permute-start(bf16[64,1,640]{2,0,1:T(8,128)(2,1)S(1)} %copy_bitcast_fusion), channel_id=1, source_target_pairs={{1,0},{2,1},{3,2},{4,3},{5,4},{6,5},{7,6},{0,7},{9,8},{10,9},{11,1... | collective-permute-start | bytes 245768 | tf_op jit(solution)/shard_map/ppermute | solution.py:30
  82.3 0.5 collective-permute-done.3
  82.8 1.9 %collective-permute-start.4 = (bf16[64,1,640]{2,0,1:T(8,128)(2,1)S(1)}, bf16[64,1,640]{2,0,1:T(8,128)(2,1)S(1)}, u32[]{:S(2)}, u32[]{:S(2)}) collective-permute-start(bf16[64,1,640]{2,0,1:T(8,128)(2,1)S(1)} %collective-permute-done.3), channel_id=1, source_target_pairs={{0,1},{1,2},{2,3},{3,4},{4,5},{5,6},{6,7},{7,0},{8,9},{9,10},{10,1... | collective-permute-start | bytes 245768 | tf_op jit(solution)/shard_map/ppermute | solution.py:28
  84.7 0.0 collective-permute-done.6
  84.7 5.1 %collective-permute-start.7 = (bf16[64,1,640]{2,0,1:T(8,128)(2,1)S(1)}, bf16[64,1,640]{2,0,1:T(8,128)(2,1)S(1)}, u32[]{:S(2)}, u32[]{:S(2)}) collective-permute-start(bf16[64,1,640]{2,0,1:T(8,128)(2,1)S(1)} %collective-permute-done.6), channel_id=1, source_target_pairs={{1,0},{2,1},{3,2},{4,3},{5,4},{6,5},{7,6},{0,7},{9,8},{10,9},{11,1... | collective-permute-start | bytes 245768 | tf_op jit(solution)/shard_map/ppermute | solution.py:30
  89.9 0.4 collective-permute-done.4
  90.3 1.9 %collective-permute-start.5 = (bf16[64,1,640]{2,0,1:T(8,128)(2,1)S(1)}, bf16[64,1,640]{2,0,1:T(8,128)(2,1)S(1)}, u32[]{:S(2)}, u32[]{:S(2)}) collective-permute-start(bf16[64,1,640]{2,0,1:T(8,128)(2,1)S(1)} %collective-permute-done.4), channel_id=1, source_target_pairs={{0,1},{1,2},{2,3},{3,4},{4,5},{5,6},{6,7},{7,0},{8,9},{9,10},{10,1... | collective-permute-start | bytes 245768 | tf_op jit(solution)/shard_map/ppermute | solution.py:28
  92.3 0.1 copy.117
  92.3 0.1 convert_element_type.140
  92.4 0.0 collective-permute-done.7
  92.5 5.3 %collective-permute-start.8 = (bf16[64,1,640]{2,0,1:T(8,128)(2,1)S(1)}, bf16[64,1,640]{2,0,1:T(8,128)(2,1)S(1)}, u32[]{:S(2)}, u32[]{:S(2)}) collective-permute-start(bf16[64,1,640]{2,0,1:T(8,128)(2,1)S(1)} %collective-permute-done.7), channel_id=1, source_target_pairs={{1,0},{2,1},{3,2},{4,3},{5,4},{6,5},{7,6},{0,7},{9,8},{10,9},{11,1... | collective-permute-start | bytes 245768 | tf_op jit(solution)/shard_map/ppermute | solution.py:30
  97.8 0.1 collective-permute-done.5
  98.0 1.6 %collective-permute-done.8 = bf16[64,1,640]{2,0,1:T(8,128)(2,1)S(1)} collective-permute-done((bf16[64,1,640]{2,0,1:T(8,128)(2,1)S(1)}, bf16[64,1,640]{2,0,1:T(8,128)(2,1)S(1)}, u32[]{:S(2)}, u32[]{:S(2)}) %collective-permute-start.8) | collective-permute-done | bytes 81952 | tf_op jit(solution)/shard_map/ppermute | solution.py:30
  99.6 0.7 gather_fusion
  100.3 0.0 all-gather.2.cloned.1.call-done
  100.3 9.8 %fusion.45 = bf16[64,4,16,10]{0,2,3,1:T(8,128)(2,1)S(1)} fusion(bf16[16,4,10,8,640]{4,3,2,1,0:T(8,128)(2,1)} %bitcast.348, bf16[8,64,640]{2,1,0:T(8,128)(2,1)S(1)} %gather_fusion), kind=kOutput, calls=%fused_computation.36 | convolution fusion | flops 419471360 | bytes 7290880 | tf_op jit(solution)/shard_map/dot_general | solution.py:195
  110.1 0.1 copy.122
  110.3 27.9 %all_gather.11 = bf16[64,64,80]{1,0,2:T(8,128)(2,1)S(1)} all-gather(bf16[64,64,10]{1,0,2:T(8,128)(2,1)S(1)} %copy.122), channel_id=1, replica_groups=mesh['z'=4,'x'=8,'core'=2,'tp'=8] {'tp'}, dimensions={2}, use_global_device_ids=true | all-gather | bytes 737280 | tf_op jit(solution)/shard_map/all_gather | solution.py:202
  138.2 1.5 copy.123
  139.7 2.9 %reshape.517 = bf16[64,5120]{1,0:T(8,128)(2,1)} reshape(bf16[64,64,80]{2,1,0:T(8,128)(2,1)S(1)} %copy.123) | data formatting | bytes 1310720 | tf_op jit(solution)/shard_map/reshape | solution.py:203
  (37 shorter events, 0.5 us)
Async XLA Ops:
  6.5 43.8 %copy-start.3 = (bf16[64,128]{1,0:T(8,128)(2,1)S(1)}, bf16[64,128]{1,0:T(8,128)(2,1)}, u32[]{:S(2)}) copy-start(bf16[64,128]{1,0:T(8,128)(2,1)} %param.10) | copy-start | bytes 49156
  6.5 48.6 %copy-start.1 = (bf16[16,128,128]{2,1,0:T(8,128)(2,1)S(1)}, bf16[16,128,128]{2,1,0:T(8,128)(2,1)}, u32[]{:S(2)}) copy-start(bf16[16,128,128]{2,1,0:T(8,128)(2,1)} %param.11) | copy-start | bytes 1572868
  6.5 93.8 %all-gather.2.cloned.1.call-start = ((), (), s32[]{:S(2)}) async-start(), calls=%async_computation.1 | async-start | bytes 6963200 | tf_op jit(solution)/shard_map/all_gather | solution.py:80
  24.2 30.9 %copy-start.2 = (bf16[16,128,128]{2,1,0:T(8,128)(2,1)S(1)}, bf16[16,128,128]{2,1,0:T(8,128)(2,1)}, u32[]{:S(2)}) copy-start(bf16[16,128,128]{2,1,0:T(8,128)(2,1)} %param.12) | copy-start | bytes 1572868
  50.8 5.2 %collective-permute-start = (bf16[64,7,128]{2,1,0:T(8,128)(2,1)S(1)}, bf16[64,7,128]{2,1,0:T(8,128)(2,1)S(1)}, u32[]{:S(2)}, u32[]{:S(2)}) collective-permute-start(bf16[64,7,128]{2,1,0:T(8,128)(2,1)S(1)} %pad_maximum_fusion.1), channel_id=1, source_target_pairs={{0,8},{8,0},{1,9},{9,1},{2,10},{10,2},{3,11},{11,3},{4,12},{12,4},... | collective-permute-start | bytes 344072 | tf_op jit(solution)/shard_map/ppermute | solution.py:38
  57.1 2.2 %copy-start = (f32[128,5,1024]{2,0,1:T(8,128)}, f32[128,5,1024]{2,0,1:T(8,128)S(1)}, u32[]{:S(2)}) copy-start(f32[128,5,1024]{2,0,1:T(8,128)S(1)} %get-tuple-element.38) | copy-start | bytes 7864324
  63.5 3.4 %collective-permute-start.1 = (bf16[64,1,5,130]{3,0,2,1:T(8,128)(2,1)S(1)}, bf16[64,1,5,130]{3,0,2,1:T(8,128)(2,1)S(1)}, u32[]{:S(2)}, u32[]{:S(2)}) collective-permute-start(bf16[64,1,5,130]{3,0,2,1:T(8,128)(2,1)S(1)} %pad_maximum_fusion), channel_id=1, source_target_pairs={{0,8},{8,0},{1,9},{9,1},{2,10},{10,2},{3,11},{11,3},{4,12},{12,4},... | collective-permute-start | bytes 249608 | tf_op jit(solution)/shard_map/ppermute | solution.py:38
  67.4 7.8 %collective-permute-start.2 = (bf16[64,1,640]{2,0,1:T(8,128)(2,1)S(1)}, bf16[64,1,640]{2,0,1:T(8,128)(2,1)S(1)}, u32[]{:S(2)}, u32[]{:S(2)}) collective-permute-start(bf16[64,1,640]{2,0,1:T(8,128)(2,1)S(1)} %copy_bitcast_fusion), channel_id=1, source_target_pairs={{0,1},{1,2},{2,3},{3,4},{4,5},{5,6},{6,7},{7,0},{8,9},{9,10},{10,1... | collective-permute-start | bytes 245768 | tf_op jit(solution)/shard_map/ppermute | solution.py:28
  75.3 7.5 %collective-permute-start.3 = (bf16[64,1,640]{2,0,1:T(8,128)(2,1)S(1)}, bf16[64,1,640]{2,0,1:T(8,128)(2,1)S(1)}, u32[]{:S(2)}, u32[]{:S(2)}) collective-permute-start(bf16[64,1,640]{2,0,1:T(8,128)(2,1)S(1)} %collective-permute-done.2), channel_id=1, source_target_pairs={{0,1},{1,2},{2,3},{3,4},{4,5},{5,6},{6,7},{7,0},{8,9},{9,10},{10,1... | collective-permute-start | bytes 245768 | tf_op jit(solution)/shard_map/ppermute | solution.py:28
  77.2 7.5 %collective-permute-start.6 = (bf16[64,1,640]{2,0,1:T(8,128)(2,1)S(1)}, bf16[64,1,640]{2,0,1:T(8,128)(2,1)S(1)}, u32[]{:S(2)}, u32[]{:S(2)}) collective-permute-start(bf16[64,1,640]{2,0,1:T(8,128)(2,1)S(1)} %copy_bitcast_fusion), channel_id=1, source_target_pairs={{1,0},{2,1},{3,2},{4,3},{5,4},{6,5},{7,6},{0,7},{9,8},{10,9},{11,1... | collective-permute-start | bytes 245768 | tf_op jit(solution)/shard_map/ppermute | solution.py:30
  82.8 7.5 %collective-permute-start.4 = (bf16[64,1,640]{2,0,1:T(8,128)(2,1)S(1)}, bf16[64,1,640]{2,0,1:T(8,128)(2,1)S(1)}, u32[]{:S(2)}, u32[]{:S(2)}) collective-permute-start(bf16[64,1,640]{2,0,1:T(8,128)(2,1)S(1)} %collective-permute-done.3), channel_id=1, source_target_pairs={{0,1},{1,2},{2,3},{3,4},{4,5},{5,6},{6,7},{7,0},{8,9},{9,10},{10,1... | collective-permute-start | bytes 245768 | tf_op jit(solution)/shard_map/ppermute | solution.py:28
  84.7 7.7 %collective-permute-start.7 = (bf16[64,1,640]{2,0,1:T(8,128)(2,1)S(1)}, bf16[64,1,640]{2,0,1:T(8,128)(2,1)S(1)}, u32[]{:S(2)}, u32[]{:S(2)}) collective-permute-start(bf16[64,1,640]{2,0,1:T(8,128)(2,1)S(1)} %collective-permute-done.6), channel_id=1, source_target_pairs={{1,0},{2,1},{3,2},{4,3},{5,4},{6,5},{7,6},{0,7},{9,8},{10,9},{11,1... | collective-permute-start | bytes 245768 | tf_op jit(solution)/shard_map/ppermute | solution.py:30
  90.3 7.5 %collective-permute-start.5 = (bf16[64,1,640]{2,0,1:T(8,128)(2,1)S(1)}, bf16[64,1,640]{2,0,1:T(8,128)(2,1)S(1)}, u32[]{:S(2)}, u32[]{:S(2)}) collective-permute-start(bf16[64,1,640]{2,0,1:T(8,128)(2,1)S(1)} %collective-permute-done.4), channel_id=1, source_target_pairs={{0,1},{1,2},{2,3},{3,4},{4,5},{5,6},{6,7},{7,0},{8,9},{9,10},{10,1... | collective-permute-start | bytes 245768 | tf_op jit(solution)/shard_map/ppermute | solution.py:28
  92.5 7.2 %collective-permute-start.8 = (bf16[64,1,640]{2,0,1:T(8,128)(2,1)S(1)}, bf16[64,1,640]{2,0,1:T(8,128)(2,1)S(1)}, u32[]{:S(2)}, u32[]{:S(2)}) collective-permute-start(bf16[64,1,640]{2,0,1:T(8,128)(2,1)S(1)} %collective-permute-done.7), channel_id=1, source_target_pairs={{1,0},{2,1},{3,2},{4,3},{5,4},{6,5},{7,6},{0,7},{9,8},{10,9},{11,1... | collective-permute-start | bytes 245768 | tf_op jit(solution)/shard_map/ppermute | solution.py:30
Sparse Core Ops, SparseCore 0:
  45.6 44.2 all-gather.1
